TPU v7x, 256 devices: a whole 4x4x8 slice. The times are simulated.
256 devices in a mesh: ctx: 32 (over z_hi, x, y), head: 8 (over z_lo, core).
Axes of the slice: x: 4, y: 4, z: 8 (z_hi: 2, z_lo: 4; z = z_hi * 4 + z_lo), core: 2. Of those that a mesh axis runs over, the one named last changes fastest.
Arguments:
- queries: bfloat16 [12288, 4096], P('ctx', 'head'), may hold values from -200 to 200
- key_matrix: bfloat16 [12288, 1024], P('ctx', 'head'), may hold values from -6 to 6
- value_matrix: bfloat16 [12288, 1024], P('ctx', 'head'), may hold values from -6 to 6
- doc_ids: int32 [12288], P('ctx'), may hold values from 0 to 15, never falling along the last dimension, each value on 1 to 6528 neighbouring positions
- out_weight: bfloat16 [4096, 4096], P('head'), may hold values from -0.09375 to 0.09375
Outputs:
- projected: bfloat16 [12288, 4096], P(('ctx', 'head'))
Inputs may be any that keep to these rules, and one draw needn't show every extreme that they name: `doc_ids`: document ids never fall along the tokens; each document has 1 to 6528 tokens and one has exactly 6528.
All inputs are finite; a program needn't handle non-finite values.
Results may differ from a plain program's by a relative error of at most 0.019.
Values may be sent and summed in bfloat16 or wider, within the bound.
No kernel may reach another device: no remote copies, remote signals or barrier semaphores. Data moves between devices by JAX's collectives and lax.ppermute only.
A program may use at most 256 MiB of HBM per device.

v0:
```python
import functools

import jax
import jax.numpy as jnp
import numpy as np
from jax import lax
from jax.experimental import pallas as pl
from jax.experimental.pallas import tpu as pltpu
from jax.sharding import Mesh, PartitionSpec as P

HEAD_WIDTH = 128
LANES = 128
MOST = 6528
DOCS = 16
NEG = -1e30
CHUNKS = 2


def attn_kernel(steps, shard_rows, heads, scale, sc_ref, q_ref, k_ref, v_ref, qs_ref, qp_ref, o_ref, m_sc, l_sc, acc_sc):
    j = pl.program_id(0)
    me = sc_ref[0]
    first = sc_ref[1]
    q_last_start = sc_ref[2]
    shard = me - (steps - 1) + j
    rows = q_ref.shape[0]

    @pl.when(j == 0)
    def _init():
        m_sc[...] = jnp.full(m_sc.shape, NEG, jnp.float32)
        l_sc[...] = jnp.zeros(l_sc.shape, jnp.float32)
        acc_sc[...] = jnp.zeros(acc_sc.shape, jnp.float32)

    def block(masked):
        k = k_ref[...]
        v = v_ref[...]
        if masked:
            k_pos = shard * shard_rows + lax.broadcasted_iota(jnp.int32, (rows, shard_rows), 1)
            allowed = (k_pos >= qs_ref[:, 0:1]) & (k_pos <= qp_ref[:, 0:1])
        for h in range(heads):
            qh = q_ref[:, h * HEAD_WIDTH:(h + 1) * HEAD_WIDTH]
            s = lax.dot_general(qh, k, (((1,), (1,)), ((), ())), preferred_element_type=jnp.float32)
            if masked:
                s = jnp.where(allowed, s, NEG)
            m_prev = m_sc[h]
            m_next = jnp.maximum(m_prev, jnp.max(s, axis=1, keepdims=True))
            p = jnp.exp((s - m_next[:, 0:1]) * scale)
            if masked:
                p = jnp.where(allowed, p, 0.0)
            alpha = jnp.exp((m_prev - m_next) * scale)
            part = p[:, 0:LANES]
            for c in range(1, shard_rows // LANES):
                part = part + p[:, c * LANES:(c + 1) * LANES]
            l_sc[h] = alpha * l_sc[h] + part
            pv = jnp.dot(p.astype(jnp.bfloat16), v, preferred_element_type=jnp.float32)
            acc_sc[h] = alpha[:, 0:1] * acc_sc[h] + pv
            m_sc[h] = m_next

    live = shard >= first
    full = (shard < me) & (shard * shard_rows >= q_last_start)

    @pl.when(live & full)
    def _full():
        block(False)

    @pl.when(live & jnp.logical_not(full))
    def _masked():
        block(True)

    @pl.when(j == steps - 1)
    def _finish():
        for h in range(heads):
            denominator = jnp.sum(l_sc[h], axis=1, keepdims=True)
            o_ref[:, h * HEAD_WIDTH:(h + 1) * HEAD_WIDTH] = (acc_sc[h] / denominator).astype(o_ref.dtype)


def attention(scalars, queries, kv, q_start, q_pos, n_xy, shard_rows):
    rows, width = queries.shape
    heads = width // HEAD_WIDTH
    steps = -(-(MOST - 1) // shard_rows) + 1
    scale = HEAD_WIDTH ** (-0.5)

    def index(j, sc, half):
        s = jnp.maximum(sc[0] - (steps - 1) + j, sc[1])
        slot = jnp.where(s // n_xy == sc[3], 0, 1)
        return (s % n_xy, slot, 0, half)

    kernel = functools.partial(attn_kernel, steps, shard_rows, heads, scale)
    return pl.pallas_call(
        kernel,
        out_shape=jax.ShapeDtypeStruct((rows, width), jnp.bfloat16),
        grid_spec=pltpu.PrefetchScalarGridSpec(
            num_scalar_prefetch=1,
            grid=(steps,),
            in_specs=[
                pl.BlockSpec((rows, width), lambda j, sc: (0, 0)),
                pl.BlockSpec((None, None, shard_rows, HEAD_WIDTH), lambda j, sc: index(j, sc, 0)),
                pl.BlockSpec((None, None, shard_rows, HEAD_WIDTH), lambda j, sc: index(j, sc, 1)),
                pl.BlockSpec((rows, LANES), lambda j, sc: (0, 0)),
                pl.BlockSpec((rows, LANES), lambda j, sc: (0, 0)),
            ],
            out_specs=pl.BlockSpec((rows, width), lambda j, sc: (0, 0)),
            scratch_shapes=[
                pltpu.VMEM((heads, rows, LANES), jnp.float32),
                pltpu.VMEM((heads, rows, LANES), jnp.float32),
                pltpu.VMEM((heads, rows, HEAD_WIDTH), jnp.float32),
            ],
        ),
        compiler_params=pltpu.CompilerParams(dimension_semantics=("arbitrary",)),
        cost_estimate=pl.CostEstimate(
            flops=4 * steps * heads * rows * shard_rows * HEAD_WIDTH,
            transcendentals=steps * heads * rows * shard_rows,
            bytes_accessed=steps * shard_rows * 2 * HEAD_WIDTH * 2 + 2 * rows * width * 2,
        ),
    )(scalars, queries, kv, kv, q_start, q_pos)


def per_device(n_xy, n_head, queries, key_matrix, value_matrix, doc_ids, out_weight):
    rows = queries.shape[0]
    zh = lax.axis_index("zh")
    me = zh * n_xy + lax.axis_index("xy")

    kv = jnp.concatenate([key_matrix, value_matrix], axis=1)
    lanes = kv.shape[1]
    tile = 8
    ids = jnp.full((tile * lanes,), -1.0, jnp.float32).at[:rows].set(doc_ids.astype(jnp.float32))
    block = jnp.concatenate([kv, ids.reshape(tile, lanes).astype(kv.dtype)], axis=0)

    partner = lax.ppermute(block, "zh", perm=[(0, 1), (1, 0)])
    pair = jnp.stack([block, partner])
    gathered = lax.all_gather(pair, "xy")

    id_rows = gathered[:, :, rows:, :].astype(jnp.float32)
    docs = jnp.arange(DOCS, dtype=jnp.float32)
    counts = jnp.sum((id_rows[..., None] == docs).astype(jnp.float32), axis=(0, 1, 2, 3))
    below = (jnp.arange(DOCS, dtype=jnp.int32)[None, :] < doc_ids[:, None]).astype(jnp.float32)
    q_start = jnp.sum(below * counts[None, :], axis=1).astype(jnp.int32)
    q_pos = me * rows + jnp.arange(rows, dtype=jnp.int32)

    per_head = rows // n_head
    piece = per_head // CHUNKS

    def chunk_of(x, c):
        x = x.reshape((n_head, CHUNKS, piece) + x.shape[1:])[:, c]
        return x.reshape((n_head * piece,) + x.shape[2:])

    outs = []
    for c in range(CHUNKS):
        qs_c = chunk_of(q_start, c)
        qp_c = chunk_of(q_pos, c)
        first = jnp.maximum(qs_c[0] // rows, 0)
        scalars = jnp.stack([me, first, qs_c[-1], zh]).astype(jnp.int32)
        attended = attention(
            scalars,
            chunk_of(queries, c),
            gathered,
            jnp.broadcast_to(qs_c[:, None], (qs_c.shape[0], LANES)),
            jnp.broadcast_to(qp_c[:, None], (qp_c.shape[0], LANES)),
            n_xy,
            rows,
        )
        projected = jnp.dot(attended, out_weight, preferred_element_type=jnp.float32).astype(jnp.bfloat16)
        outs.append(lax.psum_scatter(projected, "head", scatter_dimension=0, tiled=True))
    return jnp.concatenate(outs, axis=0)


def solution(mesh):
    n_ctx = mesh.shape["ctx"]
    n_head = mesh.shape["head"]
    n_zh = 2
    n_xy = n_ctx // n_zh
    devices = np.asarray(mesh.devices).reshape(n_zh, n_xy, n_head)
    inner = Mesh(devices, ("zh", "xy", "head"))
    ctx = ("zh", "xy")
    placed = (P(ctx, "head"), P(ctx, "head"), P(ctx, "head"), P(ctx), P("head", None))
    return jax.shard_map(
        functools.partial(per_device, n_xy, n_head),
        mesh=inner,
        in_specs=placed,
        out_specs=P(("zh", "xy", "head"), None),
        check_vma=False,
    )
```

profile of v0, /device:TPU:2, one launch (start us, length us, event | category | flops | bytes accessed | tf_op | source)
XLA Modules:
  0.0 229.7 jit_solution(10692449362674863782)
XLA Ops:
  6.5 0.0 all-gather.3.cloned.1.call-start
  6.5 0.7 convert_convert_fusion
  7.2 1.0 fusion
  8.2 7.3 %collective-permute-start = (bf16[392,256]{1,0:T(8,128)(2,1)S(1)}, bf16[392,256]{1,0:T(8,128)(2,1)S(1)}, u32[]{:S(2)}, u32[]{:S(2)}) collective-permute-start(bf16[392,256]{1,0:T(8,128)(2,1)S(1)} %get-tuple-element.24), channel_id=1, source_target_pairs={{0,128},{128,0},{1,129},{129,1},{2,130},{130,2},{3,131},{131,3},{4... | collective-permute-start | bytes 602120 | tf_op jit(solution)/shard_map/ppermute | solution.py:128
  15.5 6.0 %collective-permute-done = bf16[392,256]{1,0:T(8,128)(2,1)S(1)} collective-permute-done((bf16[392,256]{1,0:T(8,128)(2,1)S(1)}, bf16[392,256]{1,0:T(8,128)(2,1)S(1)}, u32[]{:S(2)}, u32[]{:S(2)}) %collective-permute-start) | collective-permute-done | bytes 200736 | tf_op jit(solution)/shard_map/ppermute | solution.py:128
  21.5 0.8 pad_maximum_fusion
  22.3 0.0 all-gather.3.cloned.1.call-update
  22.3 0.0 reduce-scatter.3.cloned.1.call-start
  22.4 1.8 fusion.1
  24.2 69.4 %all-gather.3.cloned.1.call-done = bf16[32,392,256]{2,1,0:T(8,128)(2,1)} async-done(((bf16[2,392,256]{2,1,0:T(8,128)(2,1)}), bf16[32,392,256]{2,1,0:T(8,128)(2,1)}) %all-gather.3.cloned.1.call-update) | async-done | bytes 6422544 | tf_op jit(solution)/shard_map/all_gather | solution.py:130
  93.6 0.9 slice_convert_fusion
  94.5 0.7 convert_reduce_fusion
  95.2 0.8 select_reduce_fusion
  95.9 0.1 convert_element_type.32
  96.1 0.1 reshape_squeeze.12
  96.2 0.6 fusion.2
  98.4 0.1 broadcast_in_dim.13
  98.5 1.2 add_add_fusion.1.sc_ref
  99.7 0.7 broadcast_in_dim.12.qs_ref
  100.5 0.7 broadcast_in_dim.14.qp_ref
  101.2 9.2 %shard_map.55 = bf16[192,512]{1,0:T(8,128)(2,1)} custom-call(s32[4]{0:T(128)} %add_add_fusion.1.sc_ref, bf16[192,512]{1,0:T(8,128)(2,1)} %bitcast.29, bf16[16,2,392,256]{3,2,1,0:T(8,128)(2,1)} %bitcast.24, bf16[16,2,392,256]{3,2,1,0:T(8,128)(2,1)} %bitcast.25, s32[192,128]{1,0:T(8,128)} %broadcast_in_dim.12.qs_ref, s32[192,128]{1,0:T(8,128)} %broadcast_in_dim.14.qp_ref), custom_call_target="tpu_custom_call" | custom-call | flops 2717908992 | bytes 3932160 | tf_op jit(solution)/shard_map/pallas_call | solution.py:88
  110.4 4.4 %convolution_convert_fusion.1 = bf16[192,4096]{1,0:T(8,128)(2,1)} fusion(bf16[192,512]{1,0:T(8,128)(2,1)} %shard_map.55, bf16[512,4096]{1,0:T(8,128)(2,1)} %param.11), kind=kOutput, calls=%fused_computation.1 | convolution fusion | flops 806092800 | bytes 5963776 | tf_op jit(solution)/shard_map/dot_general | solution.py:161
  114.8 0.0 reduce-scatter.3.cloned.1.call-update
  114.9 0.0 reduce-scatter.5.cloned.1.call-start
  114.9 0.1 reshape_squeeze.14
  115.0 0.6 fusion.3
  117.5 0.1 broadcast_in_dim.16
  117.6 1.2 add_add_fusion.2.sc_ref
  118.8 0.7 broadcast_in_dim.15.qs_ref
  119.5 0.7 broadcast_in_dim.17.qp_ref
  120.3 9.2 %shard_map.56 = bf16[192,512]{1,0:T(8,128)(2,1)} custom-call(s32[4]{0:T(128)} %add_add_fusion.2.sc_ref, bf16[192,512]{1,0:T(8,128)(2,1)} %bitcast.28, bf16[16,2,392,256]{3,2,1,0:T(8,128)(2,1)} %bitcast.26, bf16[16,2,392,256]{3,2,1,0:T(8,128)(2,1)} %bitcast.27, s32[192,128]{1,0:T(8,128)} %broadcast_in_dim.15.qs_ref, s32[192,128]{1,0:T(8,128)} %broadcast_in_dim.17.qp_ref), custom_call_target="tpu_custom_call" | custom-call | flops 2717908992 | bytes 3932160 | tf_op jit(solution)/shard_map/pallas_call | solution.py:88
  129.5 4.5 %convolution_convert_fusion = bf16[192,4096]{1,0:T(8,128)(2,1)} fusion(bf16[192,512]{1,0:T(8,128)(2,1)} %shard_map.56, bf16[512,4096]{1,0:T(8,128)(2,1)} %param.11), kind=kOutput, calls=%fused_computation | convolution fusion | flops 806092800 | bytes 5963776 | tf_op jit(solution)/shard_map/dot_general | solution.py:161
  133.9 0.0 reduce-scatter.5.cloned.1.call-update
  133.9 42.9 %reduce-scatter.3.cloned.1.call-done = bf16[24,4096]{1,0:T(8,128)(2,1)} async-done(((bf16[192,4096]{1,0:T(8,128)(2,1)}), bf16[24,4096]{1,0:T(8,128)(2,1)}) %reduce-scatter.3.cloned.1.call-update) | async-done | bytes 196624 | tf_op jit(solution)/shard_map/reduce_scatter | solution.py:162
  176.8 44.5 %reduce-scatter.5.cloned.1.call-done = bf16[24,4096]{1,0:T(8,128)(2,1)} async-done(((bf16[192,4096]{1,0:T(8,128)(2,1)}), bf16[24,4096]{1,0:T(8,128)(2,1)}) %reduce-scatter.5.cloned.1.call-update) | async-done | bytes 196624 | tf_op jit(solution)/shard_map/reduce_scatter | solution.py:162
  221.3 1.8 pad_maximum_fusion.1
  (5 shorter events, 0.1 us)
Async XLA Ops:
  6.5 87.0 %all-gather.3.cloned.1.call-start = ((), (), s32[]{:S(2)}) async-start(), calls=%async_computation.4 | async-start | bytes 6823936 | tf_op jit(solution)/shard_map/all_gather | solution.py:130
  8.2 13.3 %collective-permute-start = (bf16[392,256]{1,0:T(8,128)(2,1)S(1)}, bf16[392,256]{1,0:T(8,128)(2,1)S(1)}, u32[]{:S(2)}, u32[]{:S(2)}) collective-permute-start(bf16[392,256]{1,0:T(8,128)(2,1)S(1)} %get-tuple-element.24), channel_id=1, source_target_pairs={{0,128},{128,0},{1,129},{129,1},{2,130},{130,2},{3,131},{131,3},{4... | collective-permute-start | bytes 602120 | tf_op jit(solution)/shard_map/ppermute | solution.py:128
  22.3 154.5 %reduce-scatter.3.cloned.1.call-start = ((), (), s32[]{:S(2)}) async-start(), calls=%async_computation.2 | async-start | bytes 1769472 | tf_op jit(solution)/shard_map/reduce_scatter | solution.py:162
  114.9 106.5 %reduce-scatter.5.cloned.1.call-start = ((), (), s32[]{:S(2)}) async-start(), calls=%async_computation.3 | async-start | bytes 1769472 | tf_op jit(solution)/shard_map/reduce_scatter | solution.py:162
Sparse Core Ops, SparseCore 0:
  22.4 71.0 all-gather.2
  115.0 61.8 reduce-scatter.2
  179.4 41.8 reduce-scatter.4
where the time goes:
time: 230 us
  waiting for transfers between devices  163 us (71%)
  Pallas kernels  18.4 us (8%)
  between operations  16.8 us (7%)
  other arithmetic  9.01 us (4%)
  matrix products  8.89 us (4%)
  starting transfers between devices  7.36 us (3%)
  local copies, waits for them, and re-layouts  6.37 us (3%)
    reduce_scatter x2, waiting for transfers between devices, per_device(): lax.psum_scatter(projected, 'head', scatter_dimension=0, tiled=True)  87.4 us
    all_gather x1, waiting for transfers between devices, per_device(): gathered = lax.all_gather(pair, 'xy')  69.4 us
    pallas_call x2, Pallas kernels, attention(): pl.pallas_call(kernel, out_shape=jax.ShapeDtypeStruct((rows, width), jnp....  18.4 us
    dot_general x2, matrix products, per_device(): jnp.dot(attended, out_weight, preferred_element_type=jnp.float32)  8.89 us
    ppermute x1, starting transfers between devices, per_device(): partner = lax.ppermute(block, 'zh', perm=[(0, 1), (1, 0)])  7.28 us
    ppermute x1, waiting for transfers between devices, per_device(): partner = lax.ppermute(block, 'zh', perm=[(0, 1), (1, 0)])  6.02 us
  transfers between devices with their start and end apart: 4, of which 4 were waited for; matrix products, arithmetic and copies ran while one was open for 4% of the time, Pallas kernels for 4%

commit v1 on v0

--- a/solution.py
+++ b/solution.py
@@ -14,6 +14,7 @@
 DOCS = 16
 NEG = -1e30
 CHUNKS = 2
+SUB = 64
 
 
 def attn_kernel(steps, shard_rows, heads, scale, sc_ref, q_ref, k_ref, v_ref, qs_ref, qp_ref, o_ref, m_sc, l_sc, acc_sc):
@@ -31,17 +32,15 @@
         acc_sc[...] = jnp.zeros(acc_sc.shape, jnp.float32)
 
     def block(masked):
-        k = k_ref[...]
-        v = v_ref[...]
-        if masked:
-            k_pos = shard * shard_rows + lax.broadcasted_iota(jnp.int32, (rows, shard_rows), 1)
-            allowed = (k_pos >= qs_ref[:, 0:1]) & (k_pos <= qp_ref[:, 0:1])
-        for h in range(heads):
-            qh = q_ref[:, h * HEAD_WIDTH:(h + 1) * HEAD_WIDTH]
-            s = lax.dot_general(qh, k, (((1,), (1,)), ((), ())), preferred_element_type=jnp.float32)
+        def sub_block(h, i, carry):
+            r = pl.ds(pl.multiple_of(i * SUB, SUB), SUB)
+            qh = q_ref[r, h * HEAD_WIDTH:(h + 1) * HEAD_WIDTH]
+            s = lax.dot_general(qh, k_ref[...], (((1,), (1,)), ((), ())), preferred_element_type=jnp.float32)
             if masked:
+                k_pos = shard * shard_rows + lax.broadcasted_iota(jnp.int32, (SUB, shard_rows), 1)
+                allowed = (k_pos >= qs_ref[r, 0:1]) & (k_pos <= qp_ref[r, 0:1])
                 s = jnp.where(allowed, s, NEG)
-            m_prev = m_sc[h]
+            m_prev = m_sc[h, r, :]
             m_next = jnp.maximum(m_prev, jnp.max(s, axis=1, keepdims=True))
             p = jnp.exp((s - m_next[:, 0:1]) * scale)
             if masked:
@@ -50,10 +49,14 @@
             part = p[:, 0:LANES]
             for c in range(1, shard_rows // LANES):
                 part = part + p[:, c * LANES:(c + 1) * LANES]
-            l_sc[h] = alpha * l_sc[h] + part
-            pv = jnp.dot(p.astype(jnp.bfloat16), v, preferred_element_type=jnp.float32)
-            acc_sc[h] = alpha[:, 0:1] * acc_sc[h] + pv
-            m_sc[h] = m_next
+            l_sc[h, r, :] = alpha * l_sc[h, r, :] + part
+            pv = jnp.dot(p.astype(jnp.bfloat16), v_ref[...], preferred_element_type=jnp.float32)
+            acc_sc[h, r, :] = alpha[:, 0:1] * acc_sc[h, r, :] + pv
+            m_sc[h, r, :] = m_next
+            return carry
+
+        for h in range(heads):
+            lax.fori_loop(0, rows // SUB, functools.partial(sub_block, h), 0)
 
     live = shard >= first
     full = (shard < me) & (shard * shard_rows >= q_last_start)

time: 230 us -> 362 us (1.57)
  waiting for transfers between devices: 163 us -> 274 us
  Pallas kernels: 18.4 us -> 40.3 us
    reduce_scatter x2, waiting for transfers between devices: 87.4 us -> 198 us  [per_device(): lax.psum_scatter(projected, 'head', scatter_dimension=0, tiled=True)]
    pallas_call x2, Pallas kernels: 18.4 us -> 40.3 us  [attention(): pl.pallas_call(kernel, out_shape=jax.ShapeDtypeStruct((rows, width), jnp....]
  transfers between devices with their start and end apart: 4 -> 4, of which waited for: 4 -> 4; matrix products, arithmetic and copies ran while one was open for 4% -> 3% of each run, Pallas kernels for 4% -> 6%
where the time goes in v1:
time: 362 us; the launch traced here: 363 us
  waiting for transfers between devices  274 us (76%)
  Pallas kernels  40.3 us (11%)
  between operations  16.8 us (5%)
  other arithmetic  9.01 us (2%)
  matrix products  8.89 us (2%)
  starting transfers between devices  7.36 us (2%)
  local copies, waits for them, and re-layouts  6.37 us (2%)
    reduce_scatter x2, waiting for transfers between devices, per_device(): lax.psum_scatter(projected, 'head', scatter_dimension=0, tiled=True)  198 us
    all_gather x1, waiting for transfers between devices, per_device(): gathered = lax.all_gather(pair, 'xy')  69.4 us
    pallas_call x2, Pallas kernels, attention(): pl.pallas_call(kernel, out_shape=jax.ShapeDtypeStruct((rows, width), jnp....  40.3 us
    dot_general x2, matrix products, per_device(): jnp.dot(attended, out_weight, preferred_element_type=jnp.float32)  8.89 us
    ppermute x1, starting transfers between devices, per_device(): partner = lax.ppermute(block, 'zh', perm=[(0, 1), (1, 0)])  7.28 us
  transfers between devices with their start and end apart: 4, of which 4 were waited for; matrix products, arithmetic and copies ran while one was open for 3% of the time, Pallas kernels for 6%

profile of v1, /device:TPU:2, one launch (start us, length us, event | category | flops | bytes accessed | tf_op | source)
XLA Modules:
  0.0 362.6 jit_solution(12232984357707743721)
XLA Ops:
  6.5 0.0 all-gather.3.cloned.1.call-start
  6.5 0.7 convert_convert_fusion
  7.2 1.0 fusion
  8.2 7.3 %collective-permute-start = (bf16[392,256]{1,0:T(8,128)(2,1)S(1)}, bf16[392,256]{1,0:T(8,128)(2,1)S(1)}, u32[]{:S(2)}, u32[]{:S(2)}) collective-permute-start(bf16[392,256]{1,0:T(8,128)(2,1)S(1)} %get-tuple-element.24), channel_id=1, source_target_pairs={{0,128},{128,0},{1,129},{129,1},{2,130},{130,2},{3,131},{131,3},{4... | collective-permute-start | bytes 602120 | tf_op jit(solution)/shard_map/ppermute | solution.py:131
  15.5 6.0 %collective-permute-done = bf16[392,256]{1,0:T(8,128)(2,1)S(1)} collective-permute-done((bf16[392,256]{1,0:T(8,128)(2,1)S(1)}, bf16[392,256]{1,0:T(8,128)(2,1)S(1)}, u32[]{:S(2)}, u32[]{:S(2)}) %collective-permute-start) | collective-permute-done | bytes 200736 | tf_op jit(solution)/shard_map/ppermute | solution.py:131
  21.5 0.8 pad_maximum_fusion
  22.3 0.0 all-gather.3.cloned.1.call-update
  22.3 0.0 reduce-scatter.3.cloned.1.call-start
  22.4 1.8 fusion.1
  24.2 69.4 %all-gather.3.cloned.1.call-done = bf16[32,392,256]{2,1,0:T(8,128)(2,1)} async-done(((bf16[2,392,256]{2,1,0:T(8,128)(2,1)}), bf16[32,392,256]{2,1,0:T(8,128)(2,1)}) %all-gather.3.cloned.1.call-update) | async-done | bytes 6422544 | tf_op jit(solution)/shard_map/all_gather | solution.py:133
  93.6 0.9 slice_convert_fusion
  94.5 0.7 convert_reduce_fusion
  95.2 0.8 select_reduce_fusion
  95.9 0.1 convert_element_type.32
  96.1 0.1 reshape_squeeze.12
  96.2 0.6 fusion.2
  98.4 0.1 broadcast_in_dim.13
  98.5 1.2 add_add_fusion.1.sc_ref
  99.7 0.7 broadcast_in_dim.12.qs_ref
  100.5 0.7 broadcast_in_dim.14.qp_ref
  101.2 20.2 %shard_map.55 = bf16[192,512]{1,0:T(8,128)(2,1)} custom-call(s32[4]{0:T(128)} %add_add_fusion.1.sc_ref, bf16[192,512]{1,0:T(8,128)(2,1)} %bitcast.29, bf16[16,2,392,256]{3,2,1,0:T(8,128)(2,1)} %bitcast.24, bf16[16,2,392,256]{3,2,1,0:T(8,128)(2,1)} %bitcast.25, s32[192,128]{1,0:T(8,128)} %broadcast_in_dim.12.qs_ref, s32[192,128]{1,0:T(8,128)} %broadcast_in_dim.14.qp_ref), custom_call_target="tpu_custom_call" | custom-call | flops 2717908992 | bytes 3932160 | tf_op jit(solution)/shard_map/pallas_call | solution.py:91
  121.4 4.4 %convolution_convert_fusion.1 = bf16[192,4096]{1,0:T(8,128)(2,1)} fusion(bf16[192,512]{1,0:T(8,128)(2,1)} %shard_map.55, bf16[512,4096]{1,0:T(8,128)(2,1)} %param.11), kind=kOutput, calls=%fused_computation.1 | convolution fusion | flops 806092800 | bytes 5963776 | tf_op jit(solution)/shard_map/dot_general | solution.py:164
  125.8 0.0 reduce-scatter.3.cloned.1.call-update
  125.8 0.0 reduce-scatter.5.cloned.1.call-start
  125.9 0.1 reshape_squeeze.14
  126.0 0.6 fusion.3
  128.5 0.1 broadcast_in_dim.16
  128.6 1.2 add_add_fusion.2.sc_ref
  129.8 0.7 broadcast_in_dim.15.qs_ref
  130.5 0.7 broadcast_in_dim.17.qp_ref
  131.2 20.2 %shard_map.56 = bf16[192,512]{1,0:T(8,128)(2,1)} custom-call(s32[4]{0:T(128)} %add_add_fusion.2.sc_ref, bf16[192,512]{1,0:T(8,128)(2,1)} %bitcast.28, bf16[16,2,392,256]{3,2,1,0:T(8,128)(2,1)} %bitcast.26, bf16[16,2,392,256]{3,2,1,0:T(8,128)(2,1)} %bitcast.27, s32[192,128]{1,0:T(8,128)} %broadcast_in_dim.15.qs_ref, s32[192,128]{1,0:T(8,128)} %broadcast_in_dim.17.qp_ref), custom_call_target="tpu_custom_call" | custom-call | flops 2717908992 | bytes 3932160 | tf_op jit(solution)/shard_map/pallas_call | solution.py:91
  151.4 4.5 %convolution_convert_fusion = bf16[192,4096]{1,0:T(8,128)(2,1)} fusion(bf16[192,512]{1,0:T(8,128)(2,1)} %shard_map.56, bf16[512,4096]{1,0:T(8,128)(2,1)} %param.11), kind=kOutput, calls=%fused_computation | convolution fusion | flops 806092800 | bytes 5963776 | tf_op jit(solution)/shard_map/dot_general | solution.py:164
  155.8 0.0 reduce-scatter.5.cloned.1.call-update
  155.9 88.2 %reduce-scatter.3.cloned.1.call-done = bf16[24,4096]{1,0:T(8,128)(2,1)} async-done(((bf16[192,4096]{1,0:T(8,128)(2,1)}), bf16[24,4096]{1,0:T(8,128)(2,1)}) %reduce-scatter.3.cloned.1.call-update) | async-done | bytes 196624 | tf_op jit(solution)/shard_map/reduce_scatter | solution.py:165
  244.1 110.2 %reduce-scatter.5.cloned.1.call-done = bf16[24,4096]{1,0:T(8,128)(2,1)} async-done(((bf16[192,4096]{1,0:T(8,128)(2,1)}), bf16[24,4096]{1,0:T(8,128)(2,1)}) %reduce-scatter.5.cloned.1.call-update) | async-done | bytes 196624 | tf_op jit(solution)/shard_map/reduce_scatter | solution.py:165
  354.3 1.8 pad_maximum_fusion.1
  (5 shorter events, 0.1 us)
Async XLA Ops:
  6.5 87.0 %all-gather.3.cloned.1.call-start = ((), (), s32[]{:S(2)}) async-start(), calls=%async_computation.4 | async-start | bytes 6823936 | tf_op jit(solution)/shard_map/all_gather | solution.py:133
  8.2 13.3 %collective-permute-start = (bf16[392,256]{1,0:T(8,128)(2,1)S(1)}, bf16[392,256]{1,0:T(8,128)(2,1)S(1)}, u32[]{:S(2)}, u32[]{:S(2)}) collective-permute-start(bf16[392,256]{1,0:T(8,128)(2,1)S(1)} %get-tuple-element.24), channel_id=1, source_target_pairs={{0,128},{128,0},{1,129},{129,1},{2,130},{130,2},{3,131},{131,3},{4... | collective-permute-start | bytes 602120 | tf_op jit(solution)/shard_map/ppermute | solution.py:131
  22.3 221.8 %reduce-scatter.3.cloned.1.call-start = ((), (), s32[]{:S(2)}) async-start(), calls=%async_computation.2 | async-start | bytes 1769472 | tf_op jit(solution)/shard_map/reduce_scatter | solution.py:165
  125.8 228.5 %reduce-scatter.5.cloned.1.call-start = ((), (), s32[]{:S(2)}) async-start(), calls=%async_computation.3 | async-start | bytes 1769472 | tf_op jit(solution)/shard_map/reduce_scatter | solution.py:165
Sparse Core Ops, SparseCore 0:
  22.4 71.0 all-gather.2
  126.0 118.0 reduce-scatter.2
  246.7 107.5 reduce-scatter.4

commit v2 on v0

--- a/solution.py
+++ b/solution.py
@@ -31,27 +31,40 @@
         acc_sc[...] = jnp.zeros(acc_sc.shape, jnp.float32)
 
     def block(masked):
-        k = k_ref[...]
-        v = v_ref[...]
+        cols = shard_rows // LANES
         if masked:
-            k_pos = shard * shard_rows + lax.broadcasted_iota(jnp.int32, (rows, shard_rows), 1)
-            allowed = (k_pos >= qs_ref[:, 0:1]) & (k_pos <= qp_ref[:, 0:1])
+            lane = lax.broadcasted_iota(jnp.int32, (rows, LANES), 1)
+            allowed = []
+            for c in range(cols):
+                k_pos = shard * shard_rows + c * LANES + lane
+                allowed.append((k_pos >= qs_ref[:, 0:1]) & (k_pos <= qp_ref[:, 0:1]))
         for h in range(heads):
             qh = q_ref[:, h * HEAD_WIDTH:(h + 1) * HEAD_WIDTH]
-            s = lax.dot_general(qh, k, (((1,), (1,)), ((), ())), preferred_element_type=jnp.float32)
-            if masked:
-                s = jnp.where(allowed, s, NEG)
+            s = []
+            for c in range(cols):
+                s_c = jnp.dot(qh, k_ref[c * LANES:(c + 1) * LANES, :], preferred_element_type=jnp.float32)
+                if masked:
+                    s_c = jnp.where(allowed[c], s_c, NEG)
+                s.append(s_c)
+            top = s[0]
+            for c in range(1, cols):
+                top = jnp.maximum(top, s[c])
             m_prev = m_sc[h]
-            m_next = jnp.maximum(m_prev, jnp.max(s, axis=1, keepdims=True))
-            p = jnp.exp((s - m_next[:, 0:1]) * scale)
-            if masked:
-                p = jnp.where(allowed, p, 0.0)
+            m_next = jnp.maximum(m_prev, jnp.max(top, axis=1, keepdims=True))
+            m_b = m_next[:, 0:1]
+            part = None
+            pv = None
+            for c in range(cols):
+                p = jnp.exp((s[c] - m_b) * scale)
+                if masked:
+                    p = jnp.where(allowed[c], p, 0.0)
+                part = p if part is None else part + p
+                term = jnp.dot(
+                    p.astype(jnp.bfloat16), v_ref[c * LANES:(c + 1) * LANES, :], preferred_element_type=jnp.float32
+                )
+                pv = term if pv is None else pv + term
             alpha = jnp.exp((m_prev - m_next) * scale)
-            part = p[:, 0:LANES]
-            for c in range(1, shard_rows // LANES):
-                part = part + p[:, c * LANES:(c + 1) * LANES]
             l_sc[h] = alpha * l_sc[h] + part
-            pv = jnp.dot(p.astype(jnp.bfloat16), v, preferred_element_type=jnp.float32)
             acc_sc[h] = alpha[:, 0:1] * acc_sc[h] + pv
             m_sc[h] = m_next
 
@@ -119,7 +132,9 @@
     zh = lax.axis_index("zh")
     me = zh * n_xy + lax.axis_index("xy")
 
-    kv = jnp.concatenate([key_matrix, value_matrix], axis=1)
+    width = key_matrix.shape[1]
+    k_t = key_matrix.T.reshape(width, rows // LANES, LANES).transpose(1, 0, 2).reshape(rows, width)
+    kv = jnp.concatenate([k_t, value_matrix], axis=1)
     lanes = kv.shape[1]
     tile = 8
     ids = jnp.full((tile * lanes,), -1.0, jnp.float32).at[:rows].set(doc_ids.astype(jnp.float32))

time: 230 us -> 218 us (0.948)
  waiting for transfers between devices: 163 us -> 148 us
    reduce_scatter x2, waiting for transfers between devices: 87.4 us -> 72.4 us  [per_device(): lax.psum_scatter(projected, 'head', scatter_dimension=0, tiled=True)]
  transfers between devices with their start and end apart: 4 -> 4, of which waited for: 4 -> 4; matrix products, arithmetic and copies ran while one was open for 4% -> 4% of each run, Pallas kernels for 4% -> 5%
where the time goes in v2:
time: 218 us; the launch traced here: 217 us
  waiting for transfers between devices  148 us (68%)
  Pallas kernels  19.6 us (9%)
  between operations  16.7 us (8%)
  other arithmetic  8.89 us (4%)
  matrix products  8.89 us (4%)
  starting transfers between devices  7.36 us (3%)
  local copies, waits for them, and re-layouts  7.34 us (3%)
    reduce_scatter x2, waiting for transfers between devices, per_device(): lax.psum_scatter(projected, 'head', scatter_dimension=0, tiled=True)  72.4 us
    all_gather x1, waiting for transfers between devices, per_device(): gathered = lax.all_gather(pair, 'xy')  69.4 us
    pallas_call x2, Pallas kernels, attention(): pl.pallas_call(kernel, out_shape=jax.ShapeDtypeStruct((rows, width), jnp....  19.6 us
    dot_general x2, matrix products, per_device(): jnp.dot(attended, out_weight, preferred_element_type=jnp.float32)  8.89 us
    ppermute x1, starting transfers between devices, per_device(): partner = lax.ppermute(block, 'zh', perm=[(0, 1), (1, 0)])  7.28 us
    ppermute x1, waiting for transfers between devices, per_device(): partner = lax.ppermute(block, 'zh', perm=[(0, 1), (1, 0)])  6.02 us
  transfers between devices with their start and end apart: 4, of which 4 were waited for; matrix products, arithmetic and copies ran while one was open for 4% of the time, Pallas kernels for 5%

profile of v2, /device:TPU:2, one launch (start us, length us, event | category | flops | bytes accessed | tf_op | source)
XLA Modules:
  0.0 216.6 jit_solution(16509116908273403245)
XLA Ops:
  6.5 0.0 all-gather.3.cloned.1.call-start
  6.5 0.7 convert_convert_fusion
  7.2 1.0 copy.12
  8.3 0.9 fusion
  9.2 7.3 %collective-permute-start = (bf16[392,256]{1,0:T(8,128)(2,1)S(1)}, bf16[392,256]{1,0:T(8,128)(2,1)S(1)}, u32[]{:S(2)}, u32[]{:S(2)}) collective-permute-start(bf16[392,256]{1,0:T(8,128)(2,1)S(1)} %get-tuple-element.24), channel_id=1, source_target_pairs={{0,128},{128,0},{1,129},{129,1},{2,130},{130,2},{3,131},{131,3},{4... | collective-permute-start | bytes 602120 | tf_op jit(solution)/shard_map/ppermute | solution.py:143
  16.5 6.0 %collective-permute-done = bf16[392,256]{1,0:T(8,128)(2,1)S(1)} collective-permute-done((bf16[392,256]{1,0:T(8,128)(2,1)S(1)}, bf16[392,256]{1,0:T(8,128)(2,1)S(1)}, u32[]{:S(2)}, u32[]{:S(2)}) %collective-permute-start) | collective-permute-done | bytes 200736 | tf_op jit(solution)/shard_map/ppermute | solution.py:143
  22.5 0.8 pad_maximum_fusion
  23.3 0.0 all-gather.3.cloned.1.call-update
  23.3 0.0 reduce-scatter.5.cloned.1.call-start
  23.4 1.8 fusion.1
  25.2 69.4 %all-gather.3.cloned.1.call-done = bf16[32,392,256]{2,1,0:T(8,128)(2,1)} async-done(((bf16[2,392,256]{2,1,0:T(8,128)(2,1)}), bf16[32,392,256]{2,1,0:T(8,128)(2,1)}) %all-gather.3.cloned.1.call-update) | async-done | bytes 6422544 | tf_op jit(solution)/shard_map/all_gather | solution.py:145
  94.5 0.9 slice_convert_fusion
  95.5 0.7 convert_reduce_fusion
  96.1 0.8 select_reduce_fusion
  96.9 0.1 convert_element_type.32
  97.1 0.1 reshape_squeeze.14
  97.2 0.6 fusion.3
  99.6 0.1 broadcast_in_dim.16
  99.7 1.2 add_add_fusion.2.sc_ref
  100.8 0.7 broadcast_in_dim.15.qs_ref
  101.5 0.7 broadcast_in_dim.17.qp_ref
  102.3 9.8 %shard_map.56 = bf16[192,512]{1,0:T(8,128)(2,1)} custom-call(s32[4]{0:T(128)} %add_add_fusion.2.sc_ref, bf16[192,512]{1,0:T(8,128)(2,1)} %bitcast.35, bf16[16,2,392,256]{3,2,1,0:T(8,128)(2,1)} %bitcast.30, bf16[16,2,392,256]{3,2,1,0:T(8,128)(2,1)} %bitcast.31, s32[192,128]{1,0:T(8,128)} %broadcast_in_dim.15.qs_ref, s32[192,128]{1,0:T(8,128)} %broadcast_in_dim.17.qp_ref), custom_call_target="tpu_custom_call" | custom-call | flops 2717908992 | bytes 3932160 | tf_op jit(solution)/shard_map/pallas_call | solution.py:101
  112.1 4.4 %convolution_convert_fusion = bf16[192,4096]{1,0:T(8,128)(2,1)} fusion(bf16[192,512]{1,0:T(8,128)(2,1)} %shard_map.56, bf16[512,4096]{1,0:T(8,128)(2,1)} %param.11), kind=kOutput, calls=%fused_computation | convolution fusion | flops 806092800 | bytes 5963776 | tf_op jit(solution)/shard_map/dot_general | solution.py:176
  116.5 0.0 reduce-scatter.5.cloned.1.call-update
  116.5 0.0 reduce-scatter.3.cloned.1.call-start
  116.6 0.1 reshape_squeeze.12
  116.6 0.6 fusion.2
  118.9 0.1 broadcast_in_dim.13
  119.0 1.2 add_add_fusion.1.sc_ref
  120.1 0.7 broadcast_in_dim.12.qs_ref
  120.9 0.7 broadcast_in_dim.14.qp_ref
  121.6 9.8 %shard_map.55 = bf16[192,512]{1,0:T(8,128)(2,1)} custom-call(s32[4]{0:T(128)} %add_add_fusion.1.sc_ref, bf16[192,512]{1,0:T(8,128)(2,1)} %bitcast.34, bf16[16,2,392,256]{3,2,1,0:T(8,128)(2,1)} %bitcast.32, bf16[16,2,392,256]{3,2,1,0:T(8,128)(2,1)} %bitcast.33, s32[192,128]{1,0:T(8,128)} %broadcast_in_dim.12.qs_ref, s32[192,128]{1,0:T(8,128)} %broadcast_in_dim.14.qp_ref), custom_call_target="tpu_custom_call" | custom-call | flops 2717908992 | bytes 3932160 | tf_op jit(solution)/shard_map/pallas_call | solution.py:101
  131.4 4.5 %convolution_convert_fusion.1 = bf16[192,4096]{1,0:T(8,128)(2,1)} fusion(bf16[192,512]{1,0:T(8,128)(2,1)} %shard_map.55, bf16[512,4096]{1,0:T(8,128)(2,1)} %param.11), kind=kOutput, calls=%fused_computation.1 | convolution fusion | flops 806092800 | bytes 5963776 | tf_op jit(solution)/shard_map/dot_general | solution.py:176
  135.9 0.0 reduce-scatter.3.cloned.1.call-update
  135.9 31.7 %reduce-scatter.5.cloned.1.call-done = bf16[24,4096]{1,0:T(8,128)(2,1)} async-done(((bf16[192,4096]{1,0:T(8,128)(2,1)}), bf16[24,4096]{1,0:T(8,128)(2,1)}) %reduce-scatter.5.cloned.1.call-update) | async-done | bytes 196624 | tf_op jit(solution)/shard_map/reduce_scatter | solution.py:177
  167.6 40.7 %reduce-scatter.3.cloned.1.call-done = bf16[24,4096]{1,0:T(8,128)(2,1)} async-done(((bf16[192,4096]{1,0:T(8,128)(2,1)}), bf16[24,4096]{1,0:T(8,128)(2,1)}) %reduce-scatter.3.cloned.1.call-update) | async-done | bytes 196624 | tf_op jit(solution)/shard_map/reduce_scatter | solution.py:177
  208.3 1.8 pad_maximum_fusion.1
  (5 shorter events, 0.1 us)
Async XLA Ops:
  6.5 88.0 %all-gather.3.cloned.1.call-start = ((), (), s32[]{:S(2)}) async-start(), calls=%async_computation.4 | async-start | bytes 6823936 | tf_op jit(solution)/shard_map/all_gather | solution.py:145
  9.2 13.3 %collective-permute-start = (bf16[392,256]{1,0:T(8,128)(2,1)S(1)}, bf16[392,256]{1,0:T(8,128)(2,1)S(1)}, u32[]{:S(2)}, u32[]{:S(2)}) collective-permute-start(bf16[392,256]{1,0:T(8,128)(2,1)S(1)} %get-tuple-element.24), channel_id=1, source_target_pairs={{0,128},{128,0},{1,129},{129,1},{2,130},{130,2},{3,131},{131,3},{4... | collective-permute-start | bytes 602120 | tf_op jit(solution)/shard_map/ppermute | solution.py:143
  23.3 144.3 %reduce-scatter.5.cloned.1.call-start = ((), (), s32[]{:S(2)}) async-start(), calls=%async_computation.3 | async-start | bytes 1769472 | tf_op jit(solution)/shard_map/reduce_scatter | solution.py:177
  116.5 91.8 %reduce-scatter.3.cloned.1.call-start = ((), (), s32[]{:S(2)}) async-start(), calls=%async_computation.2 | async-start | bytes 1769472 | tf_op jit(solution)/shard_map/reduce_scatter | solution.py:177
Sparse Core Ops, SparseCore 0:
  23.4 71.0 all-gather.2
  116.6 50.9 reduce-scatter.4
  170.2 38.0 reduce-scatter.2
